TPU v7x, 512 devices: a whole 4x4x16 slice. The times are simulated.
512 devices in a mesh: seq: 64 (over x, z), tp: 8 (over y, core).
Axes of the slice: x: 4, y: 4, z: 16, core: 2. Of those that a mesh axis runs over, the one named last changes fastest.
Arguments:
- hidden_in: bfloat16 [8192, 2048], P('seq', 'tp'), may hold values from -3 to 3
- norm_gain: float32 [2048], replicated, may hold values from 0.1 to 1.9
- w_query: bfloat16 [2048, 2048], P(None, 'tp'), may hold values from -0.125 to 0.125
- w_key: bfloat16 [2048, 1024], P(None, 'tp'), may hold values from -0.125 to 0.125
- w_value: bfloat16 [2048, 1024], P(None, 'tp'), may hold values from -0.125 to 0.125
- w_headgate: bfloat16 [2048, 16], P(None, 'tp'), may hold values from -0.125 to 0.125
- w_out: bfloat16 [2048, 2048], P('tp'), may hold values from -0.125 to 0.125
- q_gain: float32 [128], replicated, may hold values from 1.5 to 4
- k_gain: float32 [128], replicated, may hold values from 0.1 to 1.9
- cache_keys: bfloat16 [2, 8192, 1024], P(None, 'seq', 'tp'), as said below
- cache_values: bfloat16 [2, 8192, 1024], P(None, 'seq', 'tp'), may hold values from -6 to 6
- cached_len: int32 [8], replicated, may hold values from 0 to 8192, as said below
- group_of: int32 [8], replicated, may hold values from 0 to 1, as said below
Outputs:
- layer_out: bfloat16 [8192, 2048], P('seq', 'tp')
Inputs may be any that keep to these rules, and one draw needn't show every extreme that they name: `cache_keys`: keys of the cached positions, of order one and larger. `cached_len`: some request attends to all 8192 cached positions of its prompt, and some to none. `group_of`: every shared prompt is used by some request.
All inputs are finite; a program needn't handle non-finite values.
Results may differ from a plain program's by a relative error of at most 0.018.
Values may be sent and summed in bfloat16 or wider, within the bound.
No kernel may reach another device: no remote copies, remote signals or barrier semaphores. Data moves between devices by JAX's collectives and lax.ppermute only.
A program may use at most 64 MiB of HBM per device.

v0:
```python
import math
import jax
import jax.numpy as jnp
from jax import lax
from jax.sharding import Mesh, PartitionSpec as P

SPAN = 1024
norm_eps = 1e-06
rope_base = 1000000.0
masked_score = -1e30


def shifted(value, axis, by):
    peers = lax.axis_size(axis)
    pairs = [(i, i + by) for i in range(peers) if 0 <= i + by < peers]
    return lax.ppermute(value, axis, pairs)


def head_norm(vec, gain):
    return vec * lax.rsqrt(jnp.mean(vec * vec, -1, keepdims=True) + norm_eps) * gain


def rotate(vec, positions):
    half = vec.shape[-1] // 2
    freq = jnp.exp(
        jnp.arange(half, dtype=jnp.float32) * (-2.0 * math.log(rope_base) / vec.shape[-1])
    )
    angle = positions.astype(jnp.float32)[:, None] * freq[None, :]
    shape_out = (vec.shape[0],) + (1,) * (vec.ndim - 2) + (half,)
    cosine = jnp.cos(angle).reshape(shape_out)
    sine = jnp.sin(angle).reshape(shape_out)
    first = vec[..., :half]
    second = vec[..., half:]
    return jnp.concatenate([first * cosine - second * sine, second * cosine + first * sine], -1)


def attend(state_now, queries, keys_block, values_block, visible):
    running_max, running_sum, running_acc = state_now
    scores = jnp.einsum(
        "tcgd,kcd->tcgk", queries, keys_block, preferred_element_type=jnp.float32
    ) * queries.shape[-1] ** (-0.5)
    scores = jnp.where(visible[:, None, None, :], scores, masked_score)
    new_max = jnp.maximum(running_max, jnp.max(scores, -1))
    rescale = jnp.exp(running_max - new_max)
    expo = jnp.exp(scores - new_max[..., None])
    new_sum = running_sum * rescale + jnp.sum(expo, -1)
    update = jnp.einsum(
        "tcgk,kcd->tcgd",
        expo.astype(jnp.bfloat16),
        values_block,
        preferred_element_type=jnp.float32,
    )
    return (new_max, new_sum, running_acc * rescale[..., None] + update)


def per_device(
    hidden_in,
    norm_gain,
    w_query,
    w_key,
    w_value,
    w_headgate,
    w_out,
    q_gain,
    k_gain,
    cache_keys,
    cache_values,
    cached_len,
    group_of,
):
    tok_rows = hidden_in.shape[0]
    head_dim = q_gain.shape[0]
    kv_local = w_key.shape[1] // head_dim
    heads_local = w_query.shape[1] // head_dim
    group_size = heads_local // kv_local
    per_request = SPAN // tok_rows
    ring_x = lax.axis_size("sx")
    ring_z = lax.axis_size("sz")
    req_count = ring_x * ring_z // per_request
    pair = ring_z // req_count
    x_index = lax.axis_index("sx")
    z_index = lax.axis_index("sz")
    seq_index = x_index * ring_z + z_index
    request = seq_index % req_count
    local_part = seq_index // req_count
    parity = z_index // req_count
    length = cached_len[request]
    peer_groups = group_of[jnp.arange(ring_z, dtype=jnp.int32) % req_count]
    cache_both = jnp.stack([cache_keys, cache_values], 1)
    incoming = lax.all_to_all(cache_both[peer_groups], "sz", 0, 0, tiled=True)
    cache_rows = ring_z * cache_keys.shape[1]
    keys_cache = incoming[:, 0].reshape(cache_rows, kv_local, head_dim)
    values_cache = incoming[:, 1].reshape(cache_rows, kv_local, head_dim)
    cache_pos = x_index * cache_rows + jnp.arange(cache_rows, dtype=jnp.int32)
    gathered = lax.all_gather(hidden_in, "tp", axis=1, tiled=True)
    widened = gathered.astype(jnp.float32)
    normed = (
        widened * lax.rsqrt(jnp.mean(widened * widened, -1, keepdims=True) + norm_eps) * norm_gain
    ).astype(jnp.bfloat16)
    positions = length + local_part * tok_rows + jnp.arange(tok_rows, dtype=jnp.int32)
    query_raw = jnp.dot(normed, w_query, preferred_element_type=jnp.float32).reshape(
        tok_rows, kv_local, group_size, head_dim
    )
    queries = rotate(head_norm(query_raw, q_gain), positions).astype(jnp.bfloat16)
    key_raw = jnp.dot(normed, w_key, preferred_element_type=jnp.float32).reshape(
        tok_rows, kv_local, head_dim
    )
    keys_new = rotate(head_norm(key_raw, k_gain), positions).astype(jnp.bfloat16)
    values_new = (
        jnp.dot(normed, w_value, preferred_element_type=jnp.float32)
        .astype(jnp.bfloat16)
        .reshape(tok_rows, kv_local, head_dim)
    )
    gates = jax.nn.sigmoid(jnp.dot(normed, w_headgate, preferred_element_type=jnp.float32)).reshape(
        tok_rows, kv_local, group_size
    )
    partner_pairs = [(z, (z + req_count) % ring_z) for z in range(ring_z)]
    partner_keys, partner_values = lax.ppermute((keys_new, values_new), "sz", partner_pairs)
    partner_part = x_index * pair + (pair - 1 - parity)
    all_queries = lax.all_gather(queries, "sx", axis=0, tiled=True)
    query_tok = (
        (jnp.arange(ring_x, dtype=jnp.int32) * pair + parity)[:, None] * tok_rows
        + jnp.arange(tok_rows, dtype=jnp.int32)[None, :]
    ).reshape(-1)
    row_ids = jnp.arange(tok_rows, dtype=jnp.int32)
    key_tok = jnp.concatenate([local_part * tok_rows + row_ids, partner_part * tok_rows + row_ids])
    keys_all = jnp.concatenate([keys_cache, keys_new, partner_keys], 0)
    values_all = jnp.concatenate([values_cache, values_new, partner_values], 0)
    query_count = query_tok.shape[0]
    visible = jnp.concatenate(
        [
            jnp.broadcast_to((cache_pos < length)[None, :], (query_count, cache_rows)),
            key_tok[None, :] <= query_tok[:, None],
        ],
        1,
    )
    scores = jnp.einsum(
        "tcgd,kcd->tcgk", all_queries, keys_all, preferred_element_type=jnp.float32
    ) * head_dim ** (-0.5)
    seen = visible[:, None, None, :]
    scores = jnp.where(seen, scores, masked_score)
    top = jnp.max(scores, -1)
    expo = jnp.where(seen, jnp.exp(scores - top[..., None]), 0.0)
    total = jnp.sum(expo, -1)
    acc = jnp.einsum(
        "tcgk,kcd->tcgd", expo.astype(jnp.bfloat16), values_all, preferred_element_type=jnp.float32
    )
    stats = jnp.stack([top, total], -1).reshape(ring_x, tok_rows, kv_local, group_size, 2)
    acc = acc.reshape(ring_x, tok_rows, kv_local, group_size, head_dim)
    stats_in = lax.all_to_all(stats, "sx", 0, 0, tiled=True)
    acc_in = lax.all_to_all(acc, "sx", 0, 0, tiled=True)
    best = jnp.max(stats_in[..., 0], 0)
    factor = jnp.exp(stats_in[..., 0] - best[None])
    total = jnp.sum(stats_in[..., 1] * factor, 0)
    summed_acc = jnp.sum(acc_in * factor[..., None], 0)
    mixed = (
        (summed_acc / total[..., None] * gates[..., None])
        .astype(jnp.bfloat16)
        .reshape(tok_rows, heads_local * head_dim)
    )
    partial_out = jnp.dot(mixed, w_out, preferred_element_type=jnp.float32)
    tp_size = lax.axis_size("tp")
    pieces = partial_out.astype(jnp.bfloat16).reshape(tok_rows, tp_size, -1)
    arrived = lax.all_to_all(pieces, "tp", 1, 1, tiled=True)
    summed = jnp.sum(arrived.astype(jnp.float32), 1)
    return (hidden_in.astype(jnp.float32) + summed).astype(jnp.bfloat16)


def solution(mesh):
    seq_size = mesh.shape["seq"]
    tp_size = mesh.shape["tp"]
    req_count = seq_size // (SPAN // 128)
    ring_z = 2 * req_count
    ring_x = seq_size // ring_z
    split_mesh = Mesh(mesh.devices.reshape(ring_x, ring_z, tp_size), ("sx", "sz", "tp"))
    seq = ("sx", "sz")
    in_specs = (
        P(seq, "tp"),
        P(),
        P(None, "tp"),
        P(None, "tp"),
        P(None, "tp"),
        P(None, "tp"),
        P("tp", None),
        P(),
        P(),
        P(None, seq, "tp"),
        P(None, seq, "tp"),
        P(),
        P(),
    )
    out_specs = P(seq, "tp")
    return jax.shard_map(
        per_device, mesh=split_mesh, in_specs=in_specs, out_specs=out_specs, check_vma=False
    )
```

profile of v0, /device:TPU:32, one launch (start us, length us, event | category | flops | bytes accessed | tf_op | source)
XLA Modules:
  0.0 155.3 jit_solution(10557558886728345072)
XLA Ops:
  0.0 14.0 %all_gather.6 = bf16[128,2048]{1,0:T(8,128)(2,1)S(1)} all-gather(bf16[128,256]{1,0:T(8,128)(2,1)} %param.13), channel_id=1, replica_groups=mesh['sx'=4,'sz'=16,'tp'=8] {'tp'}, dimensions={1}, use_global_device_ids=true | all-gather | bytes 589824 | tf_op jit(solution)/shard_map/all_gather | solution.py:95
  14.2 2.0 %fusion.10 = bf16[128,1,128]{2,0,1:T(8,128)(2,1)} fusion(bf16[2048,128]{1,0:T(8,128)(2,1)} %param.17, bf16[128,2048]{1,0:T(8,128)(2,1)S(1)} %all_gather.6, f32[2048]{0:T(1024)} %param.14, f32[128]{0:T(128)S(1)} %add_rsqrt_fusion.2), kind=kOutput, calls=%fused_computation.16 | convolution fusion | flops 68173824 | bytes 1090048 | tf_op jit(solution)/shard_map/dot_general | solution.py:110
  16.2 14.8 %collective-permute-start = (bf16[128,1,128]{2,0,1:T(8,128)(2,1)}, bf16[128,1,128]{2,0,1:T(8,128)(2,1)}, u32[]{:S(2)}, u32[]{:S(2)}) collective-permute-start(bf16[128,1,128]{2,0,1:T(8,128)(2,1)} %fusion.10), channel_id=1, source_target_pairs={{0,64},{8,72},{16,80},{24,88},{32,96},{40,104},{48,112},{56,120},{... | collective-permute-start | bytes 98312 | tf_op jit(solution)/shard_map/ppermute | solution.py:118
  31.1 1.3 gather_fusion
  32.4 0.9 pad_maximum_fusion
  33.3 1.7 %gather_fusion.1 = bf16[16,2,128,128]{3,2,1,0:T(8,128)(2,1)} fusion(bf16[2,2,128,128]{3,2,0,1:T(8,128)(2,1)S(1)} %pad_maximum_fusion, s32[1024]{0:T(1024)S(1)} %pad_clamp_fusion), kind=kCustom, calls=%fused_computation.1 | custom fusion | bytes 2097216 | tf_op jit(solution)/shard_map/gather | solution.py:90
  35.0 6.0 %all-to-all-start = ((bf16[16,2,128,128]{3,2,1,0:T(8,128)(2,1)}), bf16[16,2,128,128]{3,2,1,0:T(8,128)(2,1)S(1)}, u32[]{:S(2)}, u32[]{:S(2)}) async-start(bf16[16,2,128,128]{3,2,1,0:T(8,128)(2,1)} %gather_fusion.1), calls=%async_computation | async-start | bytes 2097152 | tf_op jit(solution)/shard_map/all_to_all | solution.py:90
  41.0 1.2 dynamic_slice.3
  42.8 1.5 multiply_reduce_fusion.2
  44.3 0.7 multiply_bitcast_fusion
  45.3 0.6 pad_maximum_fusion.2
  45.9 11.2 %collective-permute-start.1 = (bf16[128,1,128]{0,2,1:T(8,128)(2,1)}, bf16[128,1,128]{0,2,1:T(8,128)(2,1)}, u32[]{:S(2)}, u32[]{:S(2)}) collective-permute-start(bf16[128,1,128]{0,2,1:T(8,128)(2,1)} %pad_maximum_fusion.2), channel_id=1, source_target_pairs={{0,64},{8,72},{16,80},{24,88},{32,96},{40,104},{48,112},{56,120},{... | collective-permute-start | bytes 98312 | tf_op jit(solution)/shard_map/ppermute | solution.py:118
  57.1 1.6 %fusion.49 = f32[128,256]{1,0:T(8,128)S(1)} fusion(bf16[2048,256]{1,0:T(8,128)(2,1)} %param.15, bf16[128,2048]{1,0:T(8,128)(2,1)S(1)} %all_gather.6, f32[2048]{0:T(1024)} %param.14, f32[128]{0:T(128)S(1)} %add_rsqrt_fusion.2), kind=kOutput, calls=%fused_computation.98 | convolution fusion | flops 135266304 | bytes 1712640 | tf_op jit(solution)/shard_map/dot_general | solution.py:101
  60.9 2.2 %pad_add_fusion = pred[512,2304]{0,1:T(8,128)(4,1)S(1)} fusion(pred[512,256]{0,1:T(8,128)(4,1)S(1)} %broadcast_compare_fusion, pred[2304]{0:T(1024)(128)(4,1)S(1)} %pad.9.clone), kind=kLoop, calls=%fused_computation.9 | loop fusion | flops 1179648 | bytes 1313024 | tf_op jit(solution)/shard_map/concatenate | solution.py:130
  63.1 12.6 %all_gather.7 = bf16[512,1,2,128]{3,0,2,1:T(8,128)(2,1)S(1)} all-gather(bf16[128,1,2,128]{3,0,2,1:T(8,128)(2,1)S(1)} %pad_maximum_fusion.1), channel_id=1, replica_groups=mesh['sx'=4,'sz'=16,'tp'=8] {'sx'}, dimensions={0}, use_global_device_ids=true | all-gather | bytes 327680 | tf_op jit(solution)/shard_map/all_gather | solution.py:120
  75.8 1.5 copy.58
  77.2 1.5 copy.60
  78.7 1.5 copy.59
  80.1 18.6 %collective-permute-done.1 = bf16[128,1,128]{0,2,1:T(8,128)(2,1)} collective-permute-done((bf16[128,1,128]{0,2,1:T(8,128)(2,1)}, bf16[128,1,128]{0,2,1:T(8,128)(2,1)}, u32[]{:S(2)}, u32[]{:S(2)}) %collective-permute-start.1) | collective-permute-done | bytes 32800 | tf_op jit(solution)/shard_map/ppermute | solution.py:118
  98.7 1.5 copy.61
  100.2 1.1 fusion.54
  101.2 1.2 copy.72
  102.5 6.7 %fusion = (f32[512,2]{0,1:T(2,128)S(1)}, f32[2304,512,2]{1,0,2:T(8,128)}) fusion(pred[512,2304]{0,1:T(8,128)(4,1)S(1)} %pad_add_fusion, bf16[512,1,2,128]{3,0,2,1:T(8,128)(2,1)S(1)} %all_gather.7, bf16[128,1,128]{2,0,1:T(8,128)(2,1)} %copy.61, bf16[128,1,128]{2,0,1:T(8,128)(2,1)} %copy.60, bf16[2048,1,128]{2,0,1:T(8,128)(2,1)} %bitcast.102), kind=kOutput, calls=%fused_computation.4 | convolution fusion | flops 612826112 | bytes 11472896 | tf_op jit(solution)/shard_map/tcgd,kcd->tcgk/dot_general | solution.py:137
  109.3 6.1 %fusion.1 = f32[512,2]{0,1:T(2,128)S(1)} fusion(f32[2304,512,2]{1,0,2:T(8,128)} %get-tuple-element.16, f32[512,2]{0,1:T(2,128)S(1)} %get-tuple-element.15, pred[512,2304]{0,1:T(8,128)(4,1)S(1)} %pad_add_fusion), kind=kLoop, calls=%fused_computation.5 | loop fusion | flops 11795456 | bytes 10625024 | tf_op jit(solution)/shard_map/reduce_sum | solution.py:144
  115.4 0.6 copy.66
  116.0 4.3 %all-to-all-start.2 = ((f32[4,128,1,2,2]{1,3,4,2,0:T(2,128)}), f32[4,128,1,2,2]{1,3,4,2,0:T(2,128)S(1)}, u32[]{:S(2)}, u32[]{:S(2)}) async-start(f32[4,128,1,2,2]{1,3,4,2,0:T(2,128)} %copy.66), calls=%async_computation.2 | async-start | bytes 16384 | tf_op jit(solution)/shard_map/all_to_all | solution.py:150
  120.3 5.1 %fusion.7 = f32[1,2,16,4,8,128]{5,4,3,2,1,0:T(8,128)S(1)} fusion(f32[2304,512,2]{1,0,2:T(8,128)} %get-tuple-element.16, f32[512,2]{0,1:T(2,128)S(1)} %get-tuple-element.15, pred[512,2304]{0,1:T(8,128)(4,1)S(1)} %pad_add_fusion, bf16[128,1,128]{0,2,1:T(8,128)(2,1)S(1)} %copy-done.3, bf16[128,1,128]{0,2,1:T(8,128)(2,1)S(1)} %copy-done.2, ...), kind=kOutput, calls=%fused_computation.14 | convolution fusion | flops 617545728 | bytes 11735040 | tf_op jit(solution)/shard_map/tcgk,kcd->tcgd/dot_general | solution.py:145
  125.4 0.8 copy.84
  126.2 4.8 %all-to-all-start.1 = ((f32[4,128,1,2,128]{1,4,3,2,0:T(8,128)}), f32[4,128,1,2,128]{1,4,3,2,0:T(8,128)S(1)}, u32[]{:S(2)}, u32[]{:S(2)}) async-start(f32[4,128,1,2,128]{1,4,3,2,0:T(8,128)} %bitcast.98), calls=%async_computation.1 | async-start | bytes 1048576 | tf_op jit(solution)/shard_map/all_to_all | solution.py:151
  131.1 9.0 %all-to-all-done.1 = f32[4,128,1,2,128]{1,4,3,2,0:T(8,128)S(1)} async-done(((f32[4,128,1,2,128]{1,4,3,2,0:T(8,128)}), f32[4,128,1,2,128]{1,4,3,2,0:T(8,128)S(1)}, u32[]{:S(2)}, u32[]{:S(2)}) %all-to-all-start.1) | async-done | bytes 524320 | tf_op jit(solution)/shard_map/all_to_all | solution.py:151
  140.6 14.0 %all_to_all.20 = bf16[128,8,256]{2,0,1:T(8,128)(2,1)S(1)} all-to-all(bf16[128,8,256]{2,0,1:T(8,128)(2,1)S(1)} %bitcast.100), channel_id=1, replica_groups=mesh['sx'=4,'sz'=16,'tp'=8] {'tp'}, dimensions={1} | all-to-all | bytes 1048576 | tf_op jit(solution)/shard_map/all_to_all | solution.py:164
  154.6 0.6 add_convert_fusion
  (54 shorter events, 3.2 us)
Async XLA Ops:
  0.0 140.2 %copy-start = (bf16[256,2048]{1,0:T(8,128)(2,1)S(1)}, bf16[256,2048]{1,0:T(8,128)(2,1)}, u32[]{:S(2)}) copy-start(bf16[256,2048]{1,0:T(8,128)(2,1)} %param.19) | copy-start | bytes 3145732
  0.0 60.6 %copy-start.5 = (f32[2048]{0:T(1024)S(1)}, f32[2048]{0:T(1024)}, u32[]{:S(2)}) copy-start(f32[2048]{0:T(1024)} %param.14) | copy-start | bytes 24580
  0.0 60.0 %copy-start.4 = (f32[128]{0:T(128)S(1)}, f32[128]{0:T(128)}, u32[]{:S(2)}) copy-start(f32[128]{0:T(128)} %param.20) | copy-start | bytes 1540
  0.0 60.6 %copy-start.6 = (bf16[2048,2]{0,1:T(2,128)(2,1)S(1)}, bf16[2048,2]{0,1:T(2,128)(2,1)}, u32[]{:S(2)}) copy-start(bf16[2048,2]{0,1:T(2,128)(2,1)} %param.18) | copy-start | bytes 24580
  16.2 62.4 %collective-permute-start = (bf16[128,1,128]{2,0,1:T(8,128)(2,1)}, bf16[128,1,128]{2,0,1:T(8,128)(2,1)}, u32[]{:S(2)}, u32[]{:S(2)}) collective-permute-start(bf16[128,1,128]{2,0,1:T(8,128)(2,1)} %fusion.10), channel_id=1, source_target_pairs={{0,64},{8,72},{16,80},{24,88},{32,96},{40,104},{48,112},{56,120},{... | collective-permute-start | bytes 98312 | tf_op jit(solution)/shard_map/ppermute | solution.py:118
  35.0 65.2 %all-to-all-start = ((bf16[16,2,128,128]{3,2,1,0:T(8,128)(2,1)}), bf16[16,2,128,128]{3,2,1,0:T(8,128)(2,1)S(1)}, u32[]{:S(2)}, u32[]{:S(2)}) async-start(bf16[16,2,128,128]{3,2,1,0:T(8,128)(2,1)} %gather_fusion.1), calls=%async_computation | async-start | bytes 2097152 | tf_op jit(solution)/shard_map/all_to_all | solution.py:90
  45.9 52.8 %collective-permute-start.1 = (bf16[128,1,128]{0,2,1:T(8,128)(2,1)}, bf16[128,1,128]{0,2,1:T(8,128)(2,1)}, u32[]{:S(2)}, u32[]{:S(2)}) collective-permute-start(bf16[128,1,128]{0,2,1:T(8,128)(2,1)} %pad_maximum_fusion.2), channel_id=1, source_target_pairs={{0,64},{8,72},{16,80},{24,88},{32,96},{40,104},{48,112},{56,120},{... | collective-permute-start | bytes 98312 | tf_op jit(solution)/shard_map/ppermute | solution.py:118
  102.5 17.8 %copy-start.2 = (bf16[128,1,128]{0,2,1:T(8,128)(2,1)S(1)}, bf16[128,1,128]{0,2,1:T(8,128)(2,1)}, u32[]{:S(2)}) copy-start(bf16[128,1,128]{0,2,1:T(8,128)(2,1)} %copy.58) | copy-start | bytes 98308
  102.5 17.8 %copy-start.3 = (bf16[128,1,128]{0,2,1:T(8,128)(2,1)S(1)}, bf16[128,1,128]{0,2,1:T(8,128)(2,1)}, u32[]{:S(2)}) copy-start(bf16[128,1,128]{0,2,1:T(8,128)(2,1)} %copy.59) | copy-start | bytes 98308
  116.0 10.2 %all-to-all-start.2 = ((f32[4,128,1,2,2]{1,3,4,2,0:T(2,128)}), f32[4,128,1,2,2]{1,3,4,2,0:T(2,128)S(1)}, u32[]{:S(2)}, u32[]{:S(2)}) async-start(f32[4,128,1,2,2]{1,3,4,2,0:T(2,128)} %copy.66), calls=%async_computation.2 | async-start | bytes 16384 | tf_op jit(solution)/shard_map/all_to_all | solution.py:150
  120.3 34.3 %copy-start.1 = (bf16[128,256]{1,0:T(8,128)(2,1)S(1)}, bf16[128,256]{1,0:T(8,128)(2,1)}, u32[]{:S(2)}) copy-start(bf16[128,256]{1,0:T(8,128)(2,1)} %param.13) | copy-start | bytes 196612
  126.2 13.9 %all-to-all-start.1 = ((f32[4,128,1,2,128]{1,4,3,2,0:T(8,128)}), f32[4,128,1,2,128]{1,4,3,2,0:T(8,128)S(1)}, u32[]{:S(2)}, u32[]{:S(2)}) async-start(f32[4,128,1,2,128]{1,4,3,2,0:T(8,128)} %bitcast.98), calls=%async_computation.1 | async-start | bytes 1048576 | tf_op jit(solution)/shard_map/all_to_all | solution.py:151
where the time goes:
time: 156 us; the launch traced here: 155 us
  starting transfers between devices  41.1 us (26%)
  blocking collectives  40.6 us (26%)
  waiting for transfers between devices  27.6 us (18%)
  matrix products  17.5 us (11%)
  local copies, waits for them, and re-layouts  14 us (9%)
  other arithmetic  13.5 us (9%)
    ppermute x2, starting transfers between devices, per_device(): lax.ppermute((keys_new, values_new), 'sz', partner_pairs)  26 us
    ppermute x2, waiting for transfers between devices, per_device(): lax.ppermute((keys_new, values_new), 'sz', partner_pairs)  18.6 us
    all_gather x1, blocking collectives, per_device(): gathered = lax.all_gather(hidden_in, 'tp', axis=1, tiled=True)  14 us
    all_to_all x1, blocking collectives, per_device(): arrived = lax.all_to_all(pieces, 'tp', 1, 1, tiled=True)  14 us
    all_gather x1, blocking collectives, per_device(): all_queries = lax.all_gather(queries, 'sx', axis=0, tiled=True)  12.6 us
    all_to_all x1, waiting for transfers between devices, per_device(): acc_in = lax.all_to_all(acc, 'sx', 0, 0, tiled=True)  9.05 us
    dot_general x1, matrix products, per_device(): jnp.einsum('tcgd,kcd->tcgk', all_queries, keys_all, preferred_element_typ...  6.72 us
    reduce_sum x1, other arithmetic, per_device(): total = jnp.sum(expo, -1)  6.14 us
  transfers between devices with their start and end apart: 5, of which 2 were waited for; matrix products, arithmetic and copies ran while one was open for 17% of the time, Pallas kernels for 0%

commit v1 on v0

--- a/solution.py
+++ b/solution.py
@@ -117,7 +117,9 @@
     partner_pairs = [(z, (z + req_count) % ring_z) for z in range(ring_z)]
     partner_keys, partner_values = lax.ppermute((keys_new, values_new), "sz", partner_pairs)
     partner_part = x_index * pair + (pair - 1 - parity)
-    all_queries = lax.all_gather(queries, "sx", axis=0, tiled=True)
+    all_queries = jnp.concatenate(
+        lax.all_to_all(jnp.stack([queries] * lax.axis_size("sx")), "sx", 0, 0), axis=0
+    )
     query_tok = (
         (jnp.arange(ring_x, dtype=jnp.int32) * pair + parity)[:, None] * tok_rows
         + jnp.arange(tok_rows, dtype=jnp.int32)[None, :]

time: 156 us -> 164 us (1.051)
  the two profiles are of different devices: /device:TPU:32 before, /device:TPU:1 now
where the time goes in v1:
time: 164 us; the launch traced here: 163 us
  blocking collectives  41.5 us (25%)
  waiting for transfers between devices  37.1 us (23%)
  starting transfers between devices  35 us (21%)
  matrix products  18.6 us (11%)
  local copies, waits for them, and re-layouts  15.6 us (10%)
  other arithmetic  13.9 us (8%)
    ppermute x2, waiting for transfers between devices, per_device(): lax.ppermute((keys_new, values_new), 'sz', partner_pairs)  27.5 us
    all_to_all x1, blocking collectives, per_device(): arrived = lax.all_to_all(pieces, 'tp', 1, 1, tiled=True)  21.5 us
    all_gather x1, blocking collectives, per_device(): gathered = lax.all_gather(hidden_in, 'tp', axis=1, tiled=True)  20 us
    ppermute x2, starting transfers between devices, per_device(): lax.ppermute((keys_new, values_new), 'sz', partner_pairs)  14 us
    all_to_all x1, starting transfers between devices, per_device(): incoming = lax.all_to_all(cache_both[peer_groups], 'sz', 0, 0, tiled=True)  10.1 us
    all_to_all x1, waiting for transfers between devices, per_device(): acc_in = lax.all_to_all(acc, 'sx', 0, 0, tiled=True)  6.88 us
    dot_general x1, matrix products, per_device(): jnp.einsum('tcgd,kcd->tcgk', all_queries, keys_all, preferred_element_typ...  6.79 us
    reduce_sum x1, other arithmetic, per_device(): total = jnp.sum(expo, -1)  6.14 us
  transfers between devices with their start and end apart: 6, of which 4 were waited for; matrix products, arithmetic and copies ran while one was open for 16% of the time, Pallas kernels for 0%

profile of v1, /device:TPU:1, one launch (start us, length us, event | category | flops | bytes accessed | tf_op | source)
XLA Modules:
  0.0 162.7 jit_solution(4308883830764503352)
XLA Ops:
  0.1 1.3 dynamic_slice.3
  2.0 20.0 %all_gather.3 = bf16[128,2048]{1,0:T(8,128)(2,1)S(1)} all-gather(bf16[128,256]{1,0:T(8,128)(2,1)} %param.13), channel_id=1, replica_groups=mesh['sx'=4,'sz'=16,'tp'=8] {'tp'}, dimensions={1}, use_global_device_ids=true | all-gather | bytes 589824 | tf_op jit(solution)/shard_map/all_gather | solution.py:95
  22.2 1.6 fusion.49
  24.4 0.9 multiply_multiply_fusion
  26.5 3.4 %all-to-all-start.1 = ((bf16[4,128,1,2,128]{4,1,3,2,0:T(8,128)(2,1)}), bf16[4,128,1,2,128]{4,1,3,2,0:T(8,128)(2,1)S(1)}, u32[]{:S(2)}, u32[]{:S(2)}) async-start(bf16[4,128,1,2,128]{4,1,3,2,0:T(8,128)(2,1)} %stack.28), calls=%async_computation.1 | async-start | bytes 524288 | tf_op jit(solution)/shard_map/all_to_all | solution.py:121
  30.0 1.3 gather_fusion
  31.3 0.9 pad_maximum_fusion
  32.2 1.7 %gather_fusion.1 = bf16[16,2,128,128]{3,2,1,0:T(8,128)(2,1)} fusion(bf16[2,2,128,128]{3,2,0,1:T(8,128)(2,1)S(1)} %pad_maximum_fusion, s32[1024]{0:T(1024)S(1)} %pad_clamp_fusion), kind=kCustom, calls=%fused_computation.1 | custom fusion | bytes 2097216 | tf_op jit(solution)/shard_map/gather | solution.py:90
  33.9 2.7 %all-to-all-done.1 = bf16[4,128,1,2,128]{4,1,3,2,0:T(8,128)(2,1)S(1)} async-done(((bf16[4,128,1,2,128]{4,1,3,2,0:T(8,128)(2,1)}), bf16[4,128,1,2,128]{4,1,3,2,0:T(8,128)(2,1)S(1)}, u32[]{:S(2)}, u32[]{:S(2)}) %all-to-all-start.1) | async-done | bytes 262176 | tf_op jit(solution)/shard_map/all_to_all | solution.py:121
  36.6 10.1 %all-to-all-start = ((bf16[16,2,128,128]{3,2,1,0:T(8,128)(2,1)}), bf16[16,2,128,128]{3,2,1,0:T(8,128)(2,1)S(1)}, u32[]{:S(2)}, u32[]{:S(2)}) async-start(bf16[16,2,128,128]{3,2,1,0:T(8,128)(2,1)} %gather_fusion.1), calls=%async_computation | async-start | bytes 2097152 | tf_op jit(solution)/shard_map/all_to_all | solution.py:90
  46.7 2.0 %fusion.10 = bf16[128,1,128]{2,0,1:T(8,128)(2,1)} fusion(bf16[2048,128]{1,0:T(8,128)(2,1)} %param.17, bf16[128,2048]{1,0:T(8,128)(2,1)S(1)} %all_gather.3, f32[2048]{0:T(1024)S(1)} %copy-done.6, f32[128]{0:T(128)S(1)} %add_rsqrt_fusion.2), kind=kOutput, calls=%fused_computation.16 | convolution fusion | flops 68173824 | bytes 1090048 | tf_op jit(solution)/shard_map/dot_general | solution.py:110
  48.7 12.0 %collective-permute-start = (bf16[128,1,128]{2,0,1:T(8,128)(2,1)}, bf16[128,1,128]{2,0,1:T(8,128)(2,1)}, u32[]{:S(2)}, u32[]{:S(2)}) collective-permute-start(bf16[128,1,128]{2,0,1:T(8,128)(2,1)} %fusion.10), channel_id=1, source_target_pairs={{0,64},{8,72},{16,80},{24,88},{32,96},{40,104},{48,112},{56,120},{... | collective-permute-start | bytes 98312 | tf_op jit(solution)/shard_map/ppermute | solution.py:118
  60.7 1.5 multiply_reduce_fusion.2
  63.1 2.0 %collective-permute-start.1 = (bf16[128,1,128]{0,2,1:T(8,128)(2,1)}, bf16[128,1,128]{0,2,1:T(8,128)(2,1)}, u32[]{:S(2)}, u32[]{:S(2)}) collective-permute-start(bf16[128,1,128]{0,2,1:T(8,128)(2,1)} %pad_maximum_fusion.2), channel_id=1, source_target_pairs={{0,64},{8,72},{16,80},{24,88},{32,96},{40,104},{48,112},{56,120},{... | collective-permute-start | bytes 98312 | tf_op jit(solution)/shard_map/ppermute | solution.py:118
  66.0 2.2 %pad_add_fusion = pred[512,2304]{0,1:T(8,128)(4,1)S(1)} fusion(pred[512,256]{0,1:T(8,128)(4,1)S(1)} %broadcast_compare_fusion, pred[2304]{0:T(1024)(128)(4,1)S(1)} %pad.9.clone), kind=kLoop, calls=%fused_computation.9 | loop fusion | flops 1179648 | bytes 1313024 | tf_op jit(solution)/shard_map/concatenate | solution.py:132
  68.2 1.4 fusion.13
  69.5 1.5 copy.73
  71.0 1.5 copy.75
  72.5 26.3 %collective-permute-done = bf16[128,1,128]{2,0,1:T(8,128)(2,1)} collective-permute-done((bf16[128,1,128]{2,0,1:T(8,128)(2,1)}, bf16[128,1,128]{2,0,1:T(8,128)(2,1)}, u32[]{:S(2)}, u32[]{:S(2)}) %collective-permute-start) | collective-permute-done | bytes 32800 | tf_op jit(solution)/shard_map/ppermute | solution.py:118
  98.8 1.5 copy.74
  100.3 1.2 collective-permute-done.1
  101.5 1.5 copy.76
  103.7 1.1 fusion.54
  104.8 1.2 copy.89
  106.0 6.8 %fusion = (f32[512,2]{0,1:T(2,128)S(1)}, f32[2304,512,2]{1,0,2:T(8,128)}) fusion(pred[512,2304]{0,1:T(8,128)(4,1)S(1)} %pad_add_fusion, bf16[512,2,128]{2,0,1:T(8,128)(2,1)} %bitcast.105, bf16[128,1,128]{2,0,1:T(8,128)(2,1)} %copy.76, bf16[128,1,128]{2,0,1:T(8,128)(2,1)} %copy.75, bf16[2048,1,128]{2,0,1:T(8,128)(2,1)} %bitcast.103), kind=kOutput, calls=%fused_computation.4 | convolution fusion | flops 612826112 | bytes 11472896 | tf_op jit(solution)/shard_map/tcgd,kcd->tcgk/dot_general | solution.py:139
  112.9 6.1 %fusion.1 = f32[512,2]{0,1:T(2,128)S(1)} fusion(f32[2304,512,2]{1,0,2:T(8,128)} %get-tuple-element.16, f32[512,2]{0,1:T(2,128)S(1)} %get-tuple-element.15, pred[512,2304]{0,1:T(8,128)(4,1)S(1)} %pad_add_fusion), kind=kLoop, calls=%fused_computation.5 | loop fusion | flops 11795456 | bytes 10625024 | tf_op jit(solution)/shard_map/reduce_sum | solution.py:146
  119.6 3.3 %all-to-all-start.3 = ((f32[4,128,1,2,2]{1,3,4,2,0:T(2,128)}), f32[4,128,1,2,2]{1,3,4,2,0:T(2,128)S(1)}, u32[]{:S(2)}, u32[]{:S(2)}) async-start(f32[4,128,1,2,2]{1,3,4,2,0:T(2,128)} %copy.83), calls=%async_computation.3 | async-start | bytes 16384 | tf_op jit(solution)/shard_map/all_to_all | solution.py:152
  122.9 5.1 %fusion.7 = f32[1,2,16,4,8,128]{5,4,3,2,1,0:T(8,128)S(1)} fusion(f32[2304,512,2]{1,0,2:T(8,128)} %get-tuple-element.16, f32[512,2]{0,1:T(2,128)S(1)} %get-tuple-element.15, pred[512,2304]{0,1:T(8,128)(4,1)S(1)} %pad_add_fusion, bf16[128,1,128]{0,2,1:T(8,128)(2,1)S(1)} %copy-done.4, bf16[128,1,128]{0,2,1:T(8,128)(2,1)S(1)} %copy-done.3, ...), kind=kOutput, calls=%fused_computation.14 | convolution fusion | flops 617545728 | bytes 11735040 | tf_op jit(solution)/shard_map/tcgk,kcd->tcgd/dot_general | solution.py:147
  128.0 0.8 copy.99
  128.8 4.2 %all-to-all-start.2 = ((f32[4,128,1,2,128]{1,4,3,2,0:T(8,128)}), f32[4,128,1,2,128]{1,4,3,2,0:T(8,128)S(1)}, u32[]{:S(2)}, u32[]{:S(2)}) async-start(f32[4,128,1,2,128]{1,4,3,2,0:T(8,128)} %bitcast.99), calls=%async_computation.2 | async-start | bytes 1048576 | tf_op jit(solution)/shard_map/all_to_all | solution.py:153
  133.1 6.9 %all-to-all-done.2 = f32[4,128,1,2,128]{1,4,3,2,0:T(8,128)S(1)} async-done(((f32[4,128,1,2,128]{1,4,3,2,0:T(8,128)}), f32[4,128,1,2,128]{1,4,3,2,0:T(8,128)S(1)}, u32[]{:S(2)}, u32[]{:S(2)}) %all-to-all-start.2) | async-done | bytes 524320 | tf_op jit(solution)/shard_map/all_to_all | solution.py:153
  140.5 21.5 %all_to_all.25 = bf16[128,8,256]{2,0,1:T(8,128)(2,1)S(1)} all-to-all(bf16[128,8,256]{2,0,1:T(8,128)(2,1)S(1)} %bitcast.101), channel_id=1, replica_groups=mesh['sx'=4,'sz'=16,'tp'=8] {'tp'}, dimensions={1} | all-to-all | bytes 1048576 | tf_op jit(solution)/shard_map/all_to_all | solution.py:166
  (57 shorter events, 6.4 us)
Async XLA Ops:
  0.0 140.1 %copy-start = (bf16[256,2048]{1,0:T(8,128)(2,1)S(1)}, bf16[256,2048]{1,0:T(8,128)(2,1)}, u32[]{:S(2)}) copy-start(bf16[256,2048]{1,0:T(8,128)(2,1)} %param.19) | copy-start | bytes 3145732
  0.0 46.7 %copy-start.6 = (f32[2048]{0:T(1024)S(1)}, f32[2048]{0:T(1024)}, u32[]{:S(2)}) copy-start(f32[2048]{0:T(1024)} %param.14) | copy-start | bytes 24580
  0.0 62.1 %copy-start.5 = (f32[128]{0:T(128)S(1)}, f32[128]{0:T(128)}, u32[]{:S(2)}) copy-start(f32[128]{0:T(128)} %param.21) | copy-start | bytes 1540
  22.0 43.8 %copy-start.1 = (bf16[128,2048]{1,0:T(8,128)(2,1)}, bf16[128,2048]{1,0:T(8,128)(2,1)S(1)}, u32[]{:S(2)}) copy-start(bf16[128,2048]{1,0:T(8,128)(2,1)S(1)} %all_gather.3) | copy-start | bytes 1572868
  26.5 10.0 %all-to-all-start.1 = ((bf16[4,128,1,2,128]{4,1,3,2,0:T(8,128)(2,1)}), bf16[4,128,1,2,128]{4,1,3,2,0:T(8,128)(2,1)S(1)}, u32[]{:S(2)}, u32[]{:S(2)}) async-start(bf16[4,128,1,2,128]{4,1,3,2,0:T(8,128)(2,1)} %stack.28), calls=%async_computation.1 | async-start | bytes 524288 | tf_op jit(solution)/shard_map/all_to_all | solution.py:121
  36.6 67.2 %all-to-all-start = ((bf16[16,2,128,128]{3,2,1,0:T(8,128)(2,1)}), bf16[16,2,128,128]{3,2,1,0:T(8,128)(2,1)S(1)}, u32[]{:S(2)}, u32[]{:S(2)}) async-start(bf16[16,2,128,128]{3,2,1,0:T(8,128)(2,1)} %gather_fusion.1), calls=%async_computation | async-start | bytes 2097152 | tf_op jit(solution)/shard_map/all_to_all | solution.py:90
  48.7 50.1 %collective-permute-start = (bf16[128,1,128]{2,0,1:T(8,128)(2,1)}, bf16[128,1,128]{2,0,1:T(8,128)(2,1)}, u32[]{:S(2)}, u32[]{:S(2)}) collective-permute-start(bf16[128,1,128]{2,0,1:T(8,128)(2,1)} %fusion.10), channel_id=1, source_target_pairs={{0,64},{8,72},{16,80},{24,88},{32,96},{40,104},{48,112},{56,120},{... | collective-permute-start | bytes 98312 | tf_op jit(solution)/shard_map/ppermute | solution.py:118
  63.1 38.4 %collective-permute-start.1 = (bf16[128,1,128]{0,2,1:T(8,128)(2,1)}, bf16[128,1,128]{0,2,1:T(8,128)(2,1)}, u32[]{:S(2)}, u32[]{:S(2)}) collective-permute-start(bf16[128,1,128]{0,2,1:T(8,128)(2,1)} %pad_maximum_fusion.2), channel_id=1, source_target_pairs={{0,64},{8,72},{16,80},{24,88},{32,96},{40,104},{48,112},{56,120},{... | collective-permute-start | bytes 98312 | tf_op jit(solution)/shard_map/ppermute | solution.py:118
  106.0 16.9 %copy-start.3 = (bf16[128,1,128]{0,2,1:T(8,128)(2,1)S(1)}, bf16[128,1,128]{0,2,1:T(8,128)(2,1)}, u32[]{:S(2)}) copy-start(bf16[128,1,128]{0,2,1:T(8,128)(2,1)} %copy.73) | copy-start | bytes 98308
  106.0 16.9 %copy-start.4 = (bf16[128,1,128]{0,2,1:T(8,128)(2,1)S(1)}, bf16[128,1,128]{0,2,1:T(8,128)(2,1)}, u32[]{:S(2)}) copy-start(bf16[128,1,128]{0,2,1:T(8,128)(2,1)} %copy.74) | copy-start | bytes 98308
  119.6 9.2 %all-to-all-start.3 = ((f32[4,128,1,2,2]{1,3,4,2,0:T(2,128)}), f32[4,128,1,2,2]{1,3,4,2,0:T(2,128)S(1)}, u32[]{:S(2)}, u32[]{:S(2)}) async-start(f32[4,128,1,2,2]{1,3,4,2,0:T(2,128)} %copy.83), calls=%async_computation.3 | async-start | bytes 16384 | tf_op jit(solution)/shard_map/all_to_all | solution.py:152
  122.9 39.1 %copy-start.2 = (bf16[128,256]{1,0:T(8,128)(2,1)S(1)}, bf16[128,256]{1,0:T(8,128)(2,1)}, u32[]{:S(2)}) copy-start(bf16[128,256]{1,0:T(8,128)(2,1)} %param.13) | copy-start | bytes 196612
  128.8 11.2 %all-to-all-start.2 = ((f32[4,128,1,2,128]{1,4,3,2,0:T(8,128)}), f32[4,128,1,2,128]{1,4,3,2,0:T(8,128)S(1)}, u32[]{:S(2)}, u32[]{:S(2)}) async-start(f32[4,128,1,2,128]{1,4,3,2,0:T(8,128)} %bitcast.99), calls=%async_computation.2 | async-start | bytes 1048576 | tf_op jit(solution)/shard_map/all_to_all | solution.py:153
